TPU v7x, 512 devices: a whole 4x4x16 slice. The times are simulated.
512 devices in a mesh: dp: 8 (over z_hi, core), seq: 64 (over z_lo, y, x).
Axes of the slice: x: 4, y: 4, z: 16 (z_hi: 4, z_lo: 4; z = z_hi * 4 + z_lo), core: 2. Of those that a mesh axis runs over, the one named last changes fastest.
Arguments:
- query: bfloat16 [8, 8192, 512], P('dp', 'seq'), may hold values from -6 to 6
- key_in: bfloat16 [8, 8192, 128], P('dp', 'seq'), may hold values from -4.5 to 4.5
- value_in: bfloat16 [8, 8192, 128], P('dp', 'seq'), may hold values from -6 to 6
- out_gain: float32 [512], replicated, may hold values from 0.1 to 1.9
- cotangent: bfloat16 [8, 8192, 512], P('dp', 'seq'), may hold values from -6 to 6
Outputs:
- attended: bfloat16 [8, 8192, 512], P('dp', 'seq')
- grad_query: bfloat16 [8, 8192, 512], P('dp', 'seq')
- grad_key: bfloat16 [8, 8192, 128], P('dp', 'seq')
- grad_value: bfloat16 [8, 8192, 128], P('dp', 'seq')
- grad_gain: float32 [512], replicated
All inputs are finite; a program needn't handle non-finite values.
Results may differ from a plain program's by a relative error of at most 0.012.
The roundings to bfloat16 on the way count: a program that leaves them out, or rounds other values in their place, can miss the bound.
Values may be sent and summed in bfloat16 or wider, within the bound.
No kernel may reach another device: no remote copies, remote signals or barrier semaphores. Data moves between devices by JAX's collectives and lax.ppermute only.
A program may use at most 128 MiB of HBM per device.

v0:
```python
import math
import jax
import jax.numpy as jnp
from jax import lax
from jax.sharding import PartitionSpec as P

HEADS = 4
KEY = 128
VAL = 128


def to_rows(tokens, heads):
    positions = tokens.shape[0]
    width = tokens.shape[1] // heads
    return (
        tokens.reshape(positions, heads, width).transpose(1, 0, 2).reshape(heads * positions, width)
    )


def to_tokens(rows_in, heads):
    positions = rows_in.shape[0] // heads
    width = rows_in.shape[1]
    return (
        rows_in.reshape(heads, positions, width)
        .transpose(1, 0, 2)
        .reshape(positions, heads * width)
    )


def contract_first(left_mat, right_mat):
    return lax.dot_general(
        left_mat, right_mat, (((0,), (0,)), ((), ())), preferred_element_type=jnp.float32
    )


def contract_last(left_mat, right_mat):
    return lax.dot_general(
        left_mat, right_mat, (((1,), (1,)), ((), ())), preferred_element_type=jnp.float32
    )


def body(query, key_in, value_in, out_gain, cotangent):
    keys_all, values_all = (
        lax.all_gather(key_in, "seq", axis=1, tiled=True),
        lax.all_gather(value_in, "seq", axis=1, tiled=True),
    )
    key_mat = keys_all[0]
    value_mat = values_all[0]
    length = key_mat.shape[0]
    positions = query.shape[1]
    shards = lax.axis_size("seq")
    score_scale = 1.0 / math.sqrt(KEY)
    query_rows = to_rows(query[0], HEADS)
    scores = contract_last(query_rows, key_mat) * score_scale
    row_top = jnp.max(scores, axis=1, keepdims=True)
    expo_rows = jnp.exp(scores - row_top)
    weights = (expo_rows / jnp.sum(expo_rows, axis=1, keepdims=True)).astype(jnp.bfloat16)
    out_rows = jnp.dot(weights, value_mat, preferred_element_type=jnp.float32)
    out_tokens = to_tokens(out_rows, HEADS)
    attended = (out_tokens * out_gain).astype(jnp.bfloat16)
    upstream = cotangent[0].astype(jnp.float32)
    gain_total = lax.psum(jnp.sum(upstream * out_tokens, axis=0), ("dp", "seq"))
    token_total = lax.axis_size("dp") * shards * positions
    grad_gain = gain_total / math.sqrt(token_total)
    grad_out = (upstream * out_gain).astype(jnp.bfloat16)
    grad_rows = to_rows(grad_out, HEADS)
    delta_rows = jnp.sum(grad_rows.astype(jnp.float32) * out_rows, axis=1, keepdims=True)
    block_size = 2048
    block_starts = jnp.arange(length // block_size, dtype=jnp.int32) * block_size
    query_zero = jnp.zeros((query_rows.shape[0], KEY), jnp.float32)

    def score_grad(offset_at):
        key_part = lax.dynamic_slice_in_dim(key_mat, offset_at, block_size, 0)
        value_part = lax.dynamic_slice_in_dim(value_mat, offset_at, block_size, 0)
        weight_part = lax.dynamic_slice_in_dim(weights, offset_at, block_size, 1)
        d_prob = contract_last(grad_rows, value_part)
        d_score = (weight_part.astype(jnp.float32) * (d_prob - delta_rows)).astype(jnp.bfloat16)
        return (d_score, key_part, weight_part)

    def advance_both(query_acc, offset_at):
        d_score, key_part, weight_part = score_grad(offset_at)
        query_acc = query_acc + jnp.dot(d_score, key_part, preferred_element_type=jnp.float32)
        key_term = contract_first(d_score, query_rows) * score_scale
        value_term = contract_first(weight_part, grad_rows)
        return (query_acc, (key_term, value_term))

    query_acc, both_terms = lax.scan(advance_both, query_zero, block_starts)
    key_recv, value_recv = (
        lax.all_to_all(
            both_terms[0].reshape(shards, positions, KEY),
            "seq",
            split_axis=0,
            concat_axis=0,
            tiled=True,
        ),
        lax.all_to_all(
            both_terms[1].reshape(shards, positions, VAL),
            "seq",
            split_axis=0,
            concat_axis=0,
            tiled=True,
        ),
    )
    grad_key = jnp.sum(key_recv, axis=0)
    grad_value = jnp.sum(value_recv, axis=0)
    grad_query = to_tokens(query_acc * score_scale, HEADS).astype(jnp.bfloat16)
    return (
        attended[None],
        grad_query[None],
        grad_key.astype(jnp.bfloat16)[None],
        grad_value.astype(jnp.bfloat16)[None],
        grad_gain,
    )


def solution(mesh):
    placed = (
        P("dp", "seq", None),
        P("dp", "seq", None),
        P("dp", "seq", None),
        P(),
        P("dp", "seq", None),
    )
    return jax.shard_map(
        body,
        mesh=mesh,
        in_specs=placed,
        out_specs=(
            P("dp", "seq", None),
            P("dp", "seq", None),
            P("dp", "seq", None),
            P("dp", "seq", None),
            P(),
        ),
        check_vma=False,
    )
```

profile of v0, /device:TPU:1, one launch (start us, length us, event | category | flops | bytes accessed | tf_op | source)
XLA Modules:
  0.0 1053.3 jit_solution(2763086969932441278)
XLA Ops:
  10.7 312.2 %all-gather.3.cloned.1.call-done = bf16[1,8192,128]{2,1,0:T(8,128)(2,1)} async-done(((bf16[1,128,128]{2,1,0:T(8,128)(2,1)}), bf16[1,8192,128]{2,1,0:T(8,128)(2,1)}) %all-gather.3.cloned.1.call-update) | async-done | bytes 2097168 | tf_op jit(solution)/shard_map/all_gather | solution.py:44
  322.9 9.6 multiply_reduce_fusion
  332.5 8.6 fusion.8
  341.1 10.3 divide_convert_fusion
  351.5 326.2 %all-gather.5.cloned.1.call-done = bf16[1,8192,128]{2,1,0:T(8,128)(2,1)} async-done(((bf16[1,128,128]{2,1,0:T(8,128)(2,1)}), bf16[1,8192,128]{2,1,0:T(8,128)(2,1)}) %all-gather.5.cloned.1.call-update) | async-done | bytes 2097168 | tf_op jit(solution)/shard_map/all_gather | solution.py:45
  677.7 6.3 multiply_reduce_fusion.1
  684.2 77.3 %while.15 = (s32[]{:T(128)}, f32[512,128]{1,0:T(8,128)S(1)}, f32[4,2048,128]{2,1,0:T(8,128)}, f32[4,2048,128]{2,1,0:T(8,128)}, s32[4]{0:T(128)S(1)}, /*index=5*/...) while((s32[]{:T(128)}, f32[512,128]{1,0:T(8,128)S(1)}, ...), condition=%wide.region_4.0_spmd.clone, body=%wide.region_3.0_spmd.clone.sunk | while | flops 1078329344 | bytes 22939864 | solution.py:87
  686.7 2.9 constant_dynamic-slice_fusion.2
  689.6 2.5 copy.22
  692.1 3.9 fusion.40
  696.0 2.4 convolution_add_fusion.2
  698.5 3.4 fusion.41
  706.2 2.9 constant_dynamic-slice_fusion.2
  709.1 2.5 copy.22
  711.6 3.9 fusion.40
  715.5 2.5 convolution_add_fusion.2
  717.9 3.3 fusion.41
  725.4 2.9 constant_dynamic-slice_fusion.2
  728.3 2.5 copy.22
  730.9 3.9 fusion.40
  734.8 2.5 convolution_add_fusion.2
  737.2 3.3 fusion.41
  744.7 2.9 constant_dynamic-slice_fusion.2
  747.6 2.5 copy.22
  750.1 3.9 fusion.40
  754.0 2.5 convolution_add_fusion.2
  756.5 3.3 fusion.41
  761.5 60.0 %all_to_all.10 = f32[64,128,128]{2,1,0:T(8,128)} all-to-all(f32[64,128,128]{2,1,0:T(8,128)} %bitcast.85), channel_id=1, replica_groups=mesh['dp'=8,'seq'=64] {'seq'}, dimensions={0} | all-to-all | bytes 8388608 | tf_op jit(solution)/shard_map/all_to_all | solution.py:89
  821.4 5.7 all-to-all-start.1
  828.3 210.9 %psum.7 = f32[512]{0:T(512)S(1)} all-reduce(f32[512]{0:T(512)S(1)} %bitcast.95), channel_id=1, replica_groups=mesh['dp'=8,'seq'=64] {'dp','seq'}, use_global_device_ids=true, to_apply=%region_8.9 | all-reduce | flops 512 | bytes 4096 | tf_op jit(solution)/shard_map/psum | solution.py:62
  1040.4 3.0 reduce_sum.49
  1043.5 3.0 reduce_sum.50
  (30 shorter events, 15.2 us)
Async XLA Ops:
  7.2 315.7 %all-gather.3.cloned.1.call-start = ((), (), s32[]{:S(2)}) async-start(), calls=%async_computation.2 | async-start | bytes 2129920 | tf_op jit(solution)/shard_map/all_gather | solution.py:44
  7.9 669.8 %all-gather.5.cloned.1.call-start = ((), (), s32[]{:S(2)}) async-start(), calls=%async_computation.3 | async-start | bytes 2129920 | tf_op jit(solution)/shard_map/all_gather | solution.py:45
  341.1 336.5 %copy-start = (f32[512]{0:T(512)S(1)}, f32[512]{0:T(512)}, u32[]{:S(2)}) copy-start(f32[512]{0:T(512)} %param.10) | copy-start | bytes 6148
  821.4 222.0 %all-to-all-start.1 = ((f32[64,128,128]{2,1,0:T(8,128)}), f32[64,128,128]{2,1,0:T(8,128)}, u32[]{:S(2)}, u32[]{:S(2)}) async-start(f32[64,128,128]{2,1,0:T(8,128)} %bitcast.86), calls=%async_computation.1 | async-start | bytes 8388608 | tf_op jit(solution)/shard_map/all_to_all | solution.py:96
Sparse Core Ops, SparseCore 0:
  10.1 312.7 all-gather.2
  324.9 352.6 all-gather.4
where the time goes:
time: 1050 us
  waiting for transfers between devices  640 us (61%)
  blocking collectives  271 us (26%)
  matrix products  61.4 us (6%)
  local copies, waits for them, and re-layouts  27.1 us (3%)
  other arithmetic  26.4 us (3%)
  between operations  14.1 us (1%)
    all_gather x1, waiting for transfers between devices, body(): lax.all_gather(value_in, 'seq', axis=1, tiled=True)  326 us
    all_gather x1, waiting for transfers between devices, body(): lax.all_gather(key_in, 'seq', axis=1, tiled=True)  312 us
    psum x1, blocking collectives, body(): gain_total = lax.psum(jnp.sum(upstream * out_tokens, axis=0), ('dp', 'seq'))  211 us
    all_to_all x1, blocking collectives, body(): lax.all_to_all(both_terms[0].reshape(shards, positions, KEY), 'seq', spli...  60 us
    dot_general x5, matrix products, contract_last(): lax.dot_general(left_mat, right_mat, (((1,), (1,)), ((), ())), preferred_...  25.2 us
    dynamic_slice x8, local copies, waits for them, and re-layouts, score_grad(): weight_part = lax.dynamic_slice_in_dim(weights, offset_at, block_size, 1)  21.7 us
  transfers between devices with their start and end apart: 3, of which 2 were waited for; matrix products, arithmetic and copies ran while one was open for 3% of the time, Pallas kernels for 0%

commit v1 on v0

--- a/solution.py
+++ b/solution.py
@@ -41,7 +41,9 @@
 
 def body(query, key_in, value_in, out_gain, cotangent):
     keys_all, values_all = (
-        lax.all_gather(key_in, "seq", axis=1, tiled=True),
+        jnp.concatenate(
+            lax.all_to_all(jnp.stack([key_in] * lax.axis_size("seq")), "seq", 0, 0), axis=1
+        ),
         lax.all_gather(value_in, "seq", axis=1, tiled=True),
     )
     key_mat = keys_all[0]

time: 1050 us -> 713 us (0.68)
  waiting for transfers between devices: 640 us -> 284 us
  starting transfers between devices: 5.74 us -> 18.5 us
    all_gather x1 -> x0, waiting for transfers between devices: 312 us -> none  [body(): lax.all_gather(key_in, 'seq', axis=1, tiled=True)]
    all_gather x1, waiting for transfers between devices: 326 us -> 235 us  [body(): lax.all_gather(value_in, 'seq', axis=1, tiled=True)]
    all_to_all x0 -> x1, waiting for transfers between devices: none -> 48 us  [body(): lax.all_to_all(jnp.stack([key_in] * lax.axis_size('seq')), 'seq', 0, 0)]
    all_to_all x0 -> x1, starting transfers between devices: none -> 12.8 us  [body(): lax.all_to_all(jnp.stack([key_in] * lax.axis_size('seq')), 'seq', 0, 0)]
  transfers between devices with their start and end apart: 3 -> 3, of which waited for: 2 -> 2; matrix products, arithmetic and copies ran while one was open for 3% -> 5% of each run, Pallas kernels for 0% -> 0%
where the time goes in v1:
time: 713 us; the launch traced here: 712 us
  waiting for transfers between devices  284 us (40%)
  blocking collectives  271 us (38%)
  matrix products  61.4 us (9%)
  local copies, waits for them, and re-layouts  27.9 us (4%)
  other arithmetic  26.5 us (4%)
  starting transfers between devices  18.5 us (3%)
  between operations  14.2 us (2%)
  loops' own time  7.85 us (1%)
    all_gather x1, waiting for transfers between devices, body(): lax.all_gather(value_in, 'seq', axis=1, tiled=True)  235 us
    psum x1, blocking collectives, body(): gain_total = lax.psum(jnp.sum(upstream * out_tokens, axis=0), ('dp', 'seq'))  211 us
    all_to_all x1, blocking collectives, body(): lax.all_to_all(both_terms[0].reshape(shards, positions, KEY), 'seq', spli...  60 us
    all_to_all x1, waiting for transfers between devices, body(): lax.all_to_all(jnp.stack([key_in] * lax.axis_size('seq')), 'seq', 0, 0)  48 us
    dot_general x5, matrix products, contract_last(): lax.dot_general(left_mat, right_mat, (((1,), (1,)), ((), ())), preferred_...  25.2 us
    dynamic_slice x8, local copies, waits for them, and re-layouts, score_grad(): weight_part = lax.dynamic_slice_in_dim(weights, offset_at, block_size, 1)  21.7 us
    dot_general x8, matrix products, contract_first(): lax.dot_general(left_mat, right_mat, (((0,), (0,)), ((), ())), preferred_...  20.1 us
  transfers between devices with their start and end apart: 3, of which 2 were waited for; matrix products, arithmetic and copies ran while one was open for 5% of the time, Pallas kernels for 0%

profile of v1, /device:TPU:1, one launch (start us, length us, event | category | flops | bytes accessed | tf_op | source)
XLA Modules:
  0.0 711.5 jit_solution(8558143715272585328)
XLA Ops:
  7.2 2.7 stack.2
  9.8 12.8 %all-to-all-start = ((bf16[64,1,128,128]{3,2,1,0:T(8,128)(2,1)}), bf16[64,1,128,128]{3,2,1,0:T(8,128)(2,1)}, u32[]{:S(2)}, u32[]{:S(2)}) async-start(bf16[64,1,128,128]{3,2,1,0:T(8,128)(2,1)} %stack.2), calls=%async_computation | async-start | bytes 4194304 | tf_op jit(solution)/shard_map/all_to_all | solution.py:45
  23.6 48.0 %all-to-all-done = bf16[64,1,128,128]{3,2,1,0:T(8,128)(2,1)} async-done(((bf16[64,1,128,128]{3,2,1,0:T(8,128)(2,1)}), bf16[64,1,128,128]{3,2,1,0:T(8,128)(2,1)}, u32[]{:S(2)}, u32[]{:S(2)}) %all-to-all-start) | async-done | bytes 2097184 | tf_op jit(solution)/shard_map/all_to_all | solution.py:45
  71.6 9.6 %multiply_reduce_fusion = (f32[512]{0:T(512)S(1)}, f32[512,8192]{1,0:T(8,128)}) fusion(bf16[512,128]{1,0:T(8,128)(2,1)S(1)} %bitcast.80, bf16[8192,128]{1,0:T(8,128)(2,1)} %bitcast.3), kind=kOutput, calls=%fused_computation.15 | convolution fusion | flops 1082129920 | bytes 19007488 | tf_op jit(solution)/shard_map/dot_general | solution.py:37
  81.3 8.6 %fusion.8 = f32[512]{0:T(512)S(1)} fusion(f32[512,8192]{1,0:T(8,128)} %get-tuple-element.150, f32[512]{0:T(512)S(1)} %get-tuple-element.149), kind=kLoop, calls=%fused_computation.16 | loop fusion | flops 12582400 | bytes 16781312 | tf_op jit(solution)/shard_map/reduce_sum | solution.py:59
  89.9 10.3 %divide_convert_fusion = bf16[512,8192]{1,0:T(8,128)(2,1)} fusion(f32[512,8192]{1,0:T(8,128)} %get-tuple-element.150, f32[512]{0:T(512)S(1)} %fusion.8, f32[512]{0:T(512)S(1)} %get-tuple-element.149), kind=kLoop, calls=%fused_computation.13 | loop fusion | flops 16777216 | bytes 25169920 | tf_op jit(solution)/shard_map/convert_element_type | solution.py:59
  100.2 235.4 %all-gather.2.cloned.1.call-done = bf16[1,8192,128]{2,1,0:T(8,128)(2,1)} async-done(((bf16[1,128,128]{2,1,0:T(8,128)(2,1)}), bf16[1,8192,128]{2,1,0:T(8,128)(2,1)}) %all-gather.2.cloned.1.call-update) | async-done | bytes 2097168 | tf_op jit(solution)/shard_map/all_gather | solution.py:47
  335.6 6.3 multiply_reduce_fusion.1
  342.1 77.3 %while.15 = (s32[]{:T(128)}, f32[512,128]{1,0:T(8,128)S(1)}, f32[4,2048,128]{2,1,0:T(8,128)}, f32[4,2048,128]{2,1,0:T(8,128)}, s32[4]{0:T(128)S(1)}, /*index=5*/...) while((s32[]{:T(128)}, f32[512,128]{1,0:T(8,128)S(1)}, ...), condition=%wide.region_4.0_spmd.clone, body=%wide.region_3.0_spmd.clone.sunk | while | flops 1078329344 | bytes 22939864 | solution.py:89
  344.7 2.9 constant_dynamic-slice_fusion.2
  347.6 2.5 copy.28
  350.1 3.9 fusion.39
  354.0 2.5 convolution_add_fusion.2
  356.5 3.4 fusion.40
  364.1 2.9 constant_dynamic-slice_fusion.2
  367.0 2.5 copy.28
  369.6 3.9 fusion.39
  375.9 3.3 fusion.40
  383.4 2.9 constant_dynamic-slice_fusion.2
  386.3 2.5 copy.28
  388.9 3.9 fusion.39
  395.2 3.3 fusion.40
  402.7 2.9 constant_dynamic-slice_fusion.2
  405.6 2.5 copy.28
  408.1 3.9 fusion.39
  412.0 2.5 convolution_add_fusion.2
  414.5 3.3 fusion.40
  419.5 60.0 %all_to_all.15 = f32[64,128,128]{2,1,0:T(8,128)} all-to-all(f32[64,128,128]{2,1,0:T(8,128)} %bitcast.82), channel_id=1, replica_groups=mesh['dp'=8,'seq'=64] {'seq'}, dimensions={0} | all-to-all | bytes 8388608 | tf_op jit(solution)/shard_map/all_to_all | solution.py:91
  479.5 5.7 all-to-all-start.2
  486.3 211.1 %psum.7 = f32[512]{0:T(512)S(1)} all-reduce(f32[512]{0:T(512)S(1)} %bitcast.93), channel_id=1, replica_groups=mesh['dp'=8,'seq'=64] {'dp','seq'}, use_global_device_ids=true, to_apply=%region_8.9 | all-reduce | flops 512 | bytes 4096 | tf_op jit(solution)/shard_map/psum | solution.py:64
  698.6 3.0 reduce_sum.49
  701.6 3.0 reduce_sum.50
  (34 shorter events, 17.6 us)
Async XLA Ops:
  7.2 16.3 %copy-start = (bf16[1,128,512]{2,1,0:T(8,128)(2,1)S(1)}, bf16[1,128,512]{2,1,0:T(8,128)(2,1)}, u32[]{:S(2)}) copy-start(bf16[1,128,512]{2,1,0:T(8,128)(2,1)} %param.11) | copy-start | bytes 393220
  7.2 16.3 %copy-start.1 = (bf16[1,128,512]{2,1,0:T(8,128)(2,1)S(1)}, bf16[1,128,512]{2,1,0:T(8,128)(2,1)}, u32[]{:S(2)}) copy-start(bf16[1,128,512]{2,1,0:T(8,128)(2,1)} %param.7) | copy-start | bytes 393220
  9.8 61.8 %all-to-all-start = ((bf16[64,1,128,128]{3,2,1,0:T(8,128)(2,1)}), bf16[64,1,128,128]{3,2,1,0:T(8,128)(2,1)}, u32[]{:S(2)}, u32[]{:S(2)}) async-start(bf16[64,1,128,128]{3,2,1,0:T(8,128)(2,1)} %stack.2), calls=%async_computation | async-start | bytes 4194304 | tf_op jit(solution)/shard_map/all_to_all | solution.py:45
  22.7 313.0 %all-gather.2.cloned.1.call-start = ((), (), s32[]{:S(2)}) async-start(), calls=%async_computation.3 | async-start | bytes 2129920 | tf_op jit(solution)/shard_map/all_gather | solution.py:47
  89.9 245.8 %copy-start.2 = (f32[512]{0:T(512)S(1)}, f32[512]{0:T(512)}, u32[]{:S(2)}) copy-start(f32[512]{0:T(512)} %param.10) | copy-start | bytes 6148
  479.5 222.2 %all-to-all-start.2 = ((f32[64,128,128]{2,1,0:T(8,128)}), f32[64,128,128]{2,1,0:T(8,128)}, u32[]{:S(2)}, u32[]{:S(2)}) async-start(f32[64,128,128]{2,1,0:T(8,128)} %bitcast.83), calls=%async_computation.2 | async-start | bytes 8388608 | tf_op jit(solution)/shard_map/all_to_all | solution.py:98
Sparse Core Ops, SparseCore 0:
  25.5 310.0 all-gather.1
